TPU v7x, 256 devices: a whole 4x4x8 slice. The times are simulated.
256 devices in a mesh: dp: 32 (over y, z_hi, core), tensor: 8 (over z_lo, x).
Axes of the slice: x: 4, y: 4, z: 8 (z_hi: 4, z_lo: 2; z = z_hi * 2 + z_lo), core: 2. Of those that a mesh axis runs over, the one named last changes fastest.
Arguments:
- inputs: bfloat16 [32768, 2048], P(('dp', 'tensor')), may hold values from -6 to 6
- norm_gain: float32 [2048], replicated, may hold values from 0.1 to 1.9
- proj_weight: bfloat16 [2048, 3, 2048], P('dp', None, 'tensor'), may hold values from -0.125 to 0.125
- filters: float32 [3, 7, 2048], P(None, None, 'tensor'), may hold values from -2.4 to 2.4
- cotangent: bfloat16 [32768, 2048], P('dp', 'tensor'), may hold values from -18 to 18
Outputs:
- mixed: bfloat16 [32768, 2048], P('dp', 'tensor')
- grad_inputs: bfloat16 [32768, 2048], P(('dp', 'tensor'))
- grad_proj: bfloat16 [2048, 3, 2048], P('dp', None, 'tensor')
- grad_filters: float32 [3, 7, 2048], P(None, None, 'tensor')
- grad_gain: float32 [2048], replicated
All inputs are finite; a program needn't handle non-finite values.
Results may differ from a plain program's by a relative error of at most 0.02.
Values may be sent and summed in bfloat16 or wider, within the bound.
No kernel may reach another device: no remote copies, remote signals or barrier semaphores. Data moves between devices by JAX's collectives and lax.ppermute only.
A program may use at most 64 MiB of HBM per device.

v0:
```python
import jax
import jax.numpy as jnp
from jax import lax
from jax.sharding import PartitionSpec as P


def passed_along(shard, axis, by):
    size = lax.axis_size(axis)
    pairs = [(i, i + by) for i in range(size) if 0 <= i + by < size]
    return lax.ppermute(shard, axis, pairs)


def body(inputs, norm_gain, proj_weight, filters, cotangent):
    taps = filters.shape[1]
    width = taps - 1
    wide = inputs.astype(jnp.float32)
    inv_rms = lax.rsqrt(jnp.mean(wide * wide, axis=1, keepdims=True) + 1e-05)
    normed = (wide * inv_rms * norm_gain).astype(jnp.bfloat16)
    weights = lax.all_gather(proj_weight, "dp", axis=0, tiled=True)
    positions = lax.all_gather(normed, "tensor", axis=0, tiled=True)
    length = positions.shape[0]
    streams = jnp.einsum(
        "td,dsc->tsc", positions, weights, preferred_element_type=jnp.float32
    ).astype(jnp.bfloat16)
    before = passed_along(streams[length - width :], "dp", 1)
    extended = jnp.concatenate([before, streams], axis=0).astype(jnp.float32)
    conv = jnp.zeros(streams.shape, jnp.float32)
    for tap in range(taps):
        conv = conv + filters[:, tap, :] * extended[width - tap : width - tap + length]
    mixed = (conv[:, 0] * conv[:, 1] * conv[:, 2]).astype(jnp.bfloat16)
    grad_out = cotangent.astype(jnp.float32)
    grad_conv = jnp.stack(
        [
            grad_out * conv[:, 1] * conv[:, 2],
            grad_out * conv[:, 0] * conv[:, 2],
            grad_out * conv[:, 0] * conv[:, 1],
        ],
        axis=1,
    )
    after = passed_along(grad_conv[:width], "dp", -1)
    grad_extended = jnp.concatenate([grad_conv, after], axis=0)
    grad_acc = jnp.zeros(streams.shape, jnp.float32)
    for tap in range(taps):
        grad_acc = grad_acc + filters[:, tap, :] * grad_extended[tap : tap + length]
    grad_streams = grad_acc.astype(jnp.bfloat16)
    filter_local = jnp.stack(
        [
            jnp.sum(grad_conv * extended[width - tap : width - tap + length], axis=0)
            for tap in range(taps)
        ],
        axis=1,
    )
    normed_terms = jnp.einsum(
        "tsc,dsc->td", grad_streams, weights, preferred_element_type=jnp.float32
    )
    grad_normed = lax.psum_scatter(
        normed_terms.astype(jnp.bfloat16), "tensor", scatter_dimension=0, tiled=True
    ).astype(jnp.float32)
    weight_terms = jnp.einsum(
        "td,tsc->dsc", positions, grad_streams, preferred_element_type=jnp.float32
    )
    grad_proj = lax.psum_scatter(
        weight_terms.astype(jnp.bfloat16), "dp", scatter_dimension=0, tiled=True
    )
    scaled = norm_gain * grad_normed
    grad_inputs = inv_rms * (
        scaled - wide * inv_rms * inv_rms * jnp.mean(scaled * wide, axis=1, keepdims=True)
    )
    gain_local = jnp.sum(grad_normed * wide * inv_rms, axis=0)
    grad_filters = lax.psum(filter_local, "dp")
    grad_gain = lax.psum(gain_local, ("dp", "tensor"))
    return (mixed, grad_inputs.astype(jnp.bfloat16), grad_proj, grad_filters, grad_gain)


def solution(mesh):
    return jax.shard_map(
        body,
        mesh=mesh,
        in_specs=(
            P(("dp", "tensor"), None),
            P(),
            P("dp", None, "tensor"),
            P(None, None, "tensor"),
            P("dp", "tensor"),
        ),
        out_specs=(
            P("dp", "tensor"),
            P(("dp", "tensor"), None),
            P("dp", None, "tensor"),
            P(None, None, "tensor"),
            P(),
        ),
        check_vma=False,
    )
```

profile of v0, /device:TPU:1, one launch (start us, length us, event | category | flops | bytes accessed | tf_op | source)
XLA Modules:
  0.0 393.9 jit_solution(4973453960555978686)
XLA Ops:
  7.2 0.0 all-gather.5.cloned.1.call-start
  7.2 0.7 all-gather.5.cloned.1.call-update
  7.9 0.0 all-gather.3.cloned.1.call-start
  7.9 1.2 fusion.26
  9.2 2.0 fusion.20
  11.2 0.0 all-gather.3.cloned.1.call-update
  11.2 0.0 reduce-scatter.3.cloned.1.call-start
  11.3 1.0 fusion.30
  12.3 59.7 %all-gather.5.cloned.1.call-done = bf16[2048,3,256]{2,0,1:T(8,128)(2,1)} async-done(((bf16[64,3,256]{2,0,1:T(8,128)(2,1)}), bf16[2048,3,256]{2,0,1:T(8,128)(2,1)}) %all-gather.5.cloned.1.call-update) | async-done | bytes 3145744 | tf_op jit(solution)/shard_map/all_gather | solution.py:19
  72.0 54.9 %all-gather.3.cloned.1.call-done = bf16[1024,2048]{1,0:T(8,128)(2,1)} async-done(((bf16[128,2048]{1,0:T(8,128)(2,1)}), bf16[1024,2048]{1,0:T(8,128)(2,1)}) %all-gather.3.cloned.1.call-update) | async-done | bytes 4194320 | tf_op jit(solution)/shard_map/all_gather | solution.py:20
  126.9 6.6 %fusion.14 = bf16[1024,3,256]{2,0,1:T(8,128)(2,1)S(1)} fusion(bf16[2048,3,256]{2,0,1:T(8,128)(2,1)} %all-gather.5.cloned.1.call-done, bf16[1024,2048]{1,0:T(8,128)(2,1)} %all-gather.3.cloned.1.call-done), kind=kOutput, calls=%fused_computation.33 | convolution fusion | flops 3222011904 | bytes 8912896 | tf_op jit(solution)/shard_map/td,dsc->tsc/dot_general | solution.py:22
  133.5 4.7 %collective-permute-start = (bf16[6,3,256]{2,0,1:T(8,128)(2,1)S(1)}, bf16[6,3,256]{2,0,1:T(8,128)(2,1)S(1)}, u32[]{:S(2)}, u32[]{:S(2)}) collective-permute-start(bf16[6,3,256]{2,0,1:T(8,128)(2,1)S(1)} %slice.120), channel_id=1, source_target_pairs={{0,8},{8,16},{16,24},{24,32},{32,40},{40,48},{48,56},{56,64},{64,7... | collective-permute-start | bytes 27656 | tf_op jit(solution)/shard_map/ppermute | solution.py:10
  138.3 0.8 collective-permute-done
  139.1 0.3 maximum_convert_fusion
  139.4 0.0 copy-start.1
  139.4 2.6 multiply_add_fusion
  142.0 1.2 fusion.25
  143.2 2.9 multiply_reduce_fusion
  146.0 1.9 collective-permute-start.1
  148.0 4.8 %collective-permute-done.1 = f32[6,3,256]{2,0,1:T(8,128)S(1)} collective-permute-done((f32[6,3,256]{2,0,1:T(8,128)S(1)}, f32[6,3,256]{2,0,1:T(8,128)S(1)}, u32[]{:S(2)}, u32[]{:S(2)}) %collective-permute-start.1) | collective-permute-done | bytes 18464 | tf_op jit(solution)/shard_map/ppermute | solution.py:10
  152.8 0.2 pad_maximum_fusion
  153.0 2.7 fusion.8
  155.8 5.1 %bitcast_convert_fusion = bf16[1024,2048]{1,0:T(8,128)(2,1)} fusion(bf16[1024,3,256]{2,0,1:T(8,128)(2,1)S(1)} %fusion.8, bf16[2048,3,256]{2,0,1:T(8,128)(2,1)S(1)} %copy-done.3), kind=kOutput, calls=%fused_computation | convolution fusion | flops 3223322624 | bytes 8912896 | tf_op jit(solution)/shard_map/tsc,dsc->td/dot_general | solution.py:53
  160.8 0.0 reduce-scatter.3.cloned.1.call-update
  160.9 0.2 reduce-scatter.5.cloned.1.call-start
  161.1 7.5 %fusion.4 = bf16[2048,3,256]{2,0,1:T(8,128)(2,1)} fusion(bf16[1024,3,256]{2,0,1:T(8,128)(2,1)S(1)} %fusion.8, bf16[1024,2048]{1,0:T(8,128)(2,1)} %all-gather.3.cloned.1.call-done), kind=kOutput, calls=%fused_computation.5 | convolution fusion | flops 3222798336 | bytes 8912896 | tf_op jit(solution)/shard_map/td,tsc->dsc/dot_general | solution.py:59
  168.6 0.0 reduce-scatter.5.cloned.1.call-update
  168.7 135.1 %psum.14 = f32[3,7,256]{2,0,1:T(4,128)S(1)} all-reduce(f32[3,7,256]{2,0,1:T(4,128)S(1)} %constant_dynamic-update-slice_fusion), channel_id=1, replica_groups=mesh['dp'=32,'tensor'=8] {'dp'}, use_global_device_ids=true, to_apply=%region_11.0 | all-reduce | flops 5376 | bytes 43008 | tf_op jit(solution)/shard_map/psum | solution.py:70
  303.8 0.6 copy.12
  304.5 1.4 fusion.29
  305.8 79.3 %psum.15 = f32[2048]{0:T(1024)} all-reduce(f32[2048]{0:T(1024)S(1)} %get-tuple-element.17), channel_id=1, replica_groups=mesh['dp'=32,'tensor'=8] {'dp','tensor'}, use_global_device_ids=true, to_apply=%region_13.0 | all-reduce | flops 2048 | bytes 16384 | tf_op jit(solution)/shard_map/psum | solution.py:71
  385.2 2.2 fusion.23
  (24 shorter events, 0.1 us)
Async XLA Ops:
  7.2 64.9 %all-gather.5.cloned.1.call-start = ((), (), s32[]{:S(2)}) async-start(), calls=%async_computation.3 | async-start | bytes 3244032 | tf_op jit(solution)/shard_map/all_gather | solution.py:19
  7.9 119.0 %all-gather.3.cloned.1.call-start = ((), (), s32[]{:S(2)}) async-start(), calls=%async_computation.2 | async-start | bytes 4718592 | tf_op jit(solution)/shard_map/all_gather | solution.py:20
  11.2 293.2 %reduce-scatter.3.cloned.1.call-start = ((), (), s32[]{:S(2)}) async-start(), calls=%async_computation.4 | async-start | bytes 4718592 | tf_op jit(solution)/shard_map/reduce_scatter | solution.py:56
  133.5 5.5 %collective-permute-start = (bf16[6,3,256]{2,0,1:T(8,128)(2,1)S(1)}, bf16[6,3,256]{2,0,1:T(8,128)(2,1)S(1)}, u32[]{:S(2)}, u32[]{:S(2)}) collective-permute-start(bf16[6,3,256]{2,0,1:T(8,128)(2,1)S(1)} %slice.120), channel_id=1, source_target_pairs={{0,8},{8,16},{16,24},{24,32},{32,40},{40,48},{48,56},{56,64},{64,7... | collective-permute-start | bytes 27656 | tf_op jit(solution)/shard_map/ppermute | solution.py:10
  139.4 2.6 copy-start.1
  146.0 6.8 %collective-permute-start.1 = (f32[6,3,256]{2,0,1:T(8,128)S(1)}, f32[6,3,256]{2,0,1:T(8,128)S(1)}, u32[]{:S(2)}, u32[]{:S(2)}) collective-permute-start(f32[6,3,256]{2,0,1:T(8,128)S(1)} %slice.131), channel_id=1, source_target_pairs={{8,0},{16,8},{24,16},{32,24},{40,32},{48,40},{56,48},{64,56},{72,6... | collective-permute-start | bytes 55304 | tf_op jit(solution)/shard_map/ppermute | solution.py:10
  153.0 2.7 copy-start.3
  160.9 226.5 %reduce-scatter.5.cloned.1.call-start = ((), (), s32[]{:S(2)}) async-start(), calls=%async_computation.5 | async-start | bytes 3244032 | tf_op jit(solution)/shard_map/reduce_scatter | solution.py:62
  168.6 135.8 %copy-start = (bf16[128,2048]{1,0:T(8,128)(2,1)S(1)}, bf16[128,2048]{1,0:T(8,128)(2,1)}, u32[]{:S(2)}) copy-start(bf16[128,2048]{1,0:T(8,128)(2,1)} %param.5) | copy-start | bytes 1572868
  168.6 135.8 %copy-start.2 = (f32[2048]{0:T(1024)S(1)}, f32[2048]{0:T(1024)}, u32[]{:S(2)}) copy-start(f32[2048]{0:T(1024)} %param.6) | copy-start | bytes 24580
Sparse Core Ops, SparseCore 0:
  10.7 61.3 all-gather.4
  74.4 52.5 all-gather.2
  161.0 54.1 reduce-scatter.2
  219.5 92.7 reduce-scatter.4
where the time goes:
time: 394 us
  blocking collectives  214 us (54%)
  waiting for transfers between devices  121 us (31%)
  matrix products  19.2 us (5%)
  other arithmetic  16.6 us (4%)
  between operations  13.9 us (4%)
  starting transfers between devices  6.99 us (2%)
    psum x1, blocking collectives, body(): grad_filters = lax.psum(filter_local, 'dp')  135 us
    psum x1, blocking collectives, body(): grad_gain = lax.psum(gain_local, ('dp', 'tensor'))  79.3 us
    all_gather x1, waiting for transfers between devices, body(): weights = lax.all_gather(proj_weight, 'dp', axis=0, tiled=True)  59.7 us
    all_gather x1, waiting for transfers between devices, body(): positions = lax.all_gather(normed, 'tensor', axis=0, tiled=True)  54.9 us
  transfers between devices with their start and end apart: 6, of which 4 were waited for; matrix products, arithmetic and copies ran while one was open for 4% of the time, Pallas kernels for 0%

commit v1 on v0

--- a/solution.py
+++ b/solution.py
@@ -68,7 +68,9 @@
     )
     gain_local = jnp.sum(grad_normed * wide * inv_rms, axis=0)
     grad_filters = lax.psum(filter_local, "dp")
-    grad_gain = lax.psum(gain_local, ("dp", "tensor"))
+    grad_gain = gain_local
+    for over in ("dp", "tensor"):
+        grad_gain = lax.psum(grad_gain, over)
     return (mixed, grad_inputs.astype(jnp.bfloat16), grad_proj, grad_filters, grad_gain)
 
 

time: 394 us -> 386 us (0.980)
  the two profiles are of different devices: /device:TPU:1 before, /device:TPU:32 now
where the time goes in v1:
time: 386 us; the launch traced here: 385 us
  waiting for transfers between devices  168 us (44%)
  blocking collectives  163 us (42%)
  matrix products  19.1 us (5%)
  other arithmetic  16.7 us (4%)
  between operations  13.9 us (4%)
    psum x1, blocking collectives, body(): grad_filters = lax.psum(filter_local, 'dp')  145 us
    all_gather x1, waiting for transfers between devices, body(): weights = lax.all_gather(proj_weight, 'dp', axis=0, tiled=True)  57 us
    all_gather x1, waiting for transfers between devices, body(): positions = lax.all_gather(normed, 'tensor', axis=0, tiled=True)  55.3 us
    reduce_scatter x1, waiting for transfers between devices, body(): lax.psum_scatter(normed_terms.astype(jnp.bfloat16), 'tensor', scatter_dim...  49.9 us
    psum x1, blocking collectives, body(): grad_gain = lax.psum(grad_gain, over)  18 us
  transfers between devices with their start and end apart: 6, of which 5 were waited for; matrix products, arithmetic and copies ran while one was open for 4% of the time, Pallas kernels for 0%

profile of v1, /device:TPU:32, one launch (start us, length us, event | category | flops | bytes accessed | tf_op | source)
XLA Modules:
  0.0 385.2 jit_solution(18349067053917959614)
XLA Ops:
  7.2 0.0 all-gather.5.cloned.1.call-start
  7.2 0.7 all-gather.5.cloned.1.call-update
  7.9 0.0 all-gather.3.cloned.1.call-start
  7.9 1.2 fusion.26
  9.2 2.0 fusion.20
  11.2 0.0 all-gather.3.cloned.1.call-update
  11.2 0.0 reduce-scatter.3.cloned.1.call-start
  11.3 1.0 fusion.30
  12.3 57.0 %all-gather.5.cloned.1.call-done = bf16[2048,3,256]{2,0,1:T(8,128)(2,1)} async-done(((bf16[64,3,256]{2,0,1:T(8,128)(2,1)}), bf16[2048,3,256]{2,0,1:T(8,128)(2,1)}) %all-gather.5.cloned.1.call-update) | async-done | bytes 3145744 | tf_op jit(solution)/shard_map/all_gather | solution.py:19
  69.3 55.3 %all-gather.3.cloned.1.call-done = bf16[1024,2048]{1,0:T(8,128)(2,1)} async-done(((bf16[128,2048]{1,0:T(8,128)(2,1)}), bf16[1024,2048]{1,0:T(8,128)(2,1)}) %all-gather.3.cloned.1.call-update) | async-done | bytes 4194320 | tf_op jit(solution)/shard_map/all_gather | solution.py:20
  124.7 6.6 %fusion.14 = bf16[1024,3,256]{2,0,1:T(8,128)(2,1)S(1)} fusion(bf16[2048,3,256]{2,0,1:T(8,128)(2,1)} %all-gather.5.cloned.1.call-done, bf16[1024,2048]{1,0:T(8,128)(2,1)} %all-gather.3.cloned.1.call-done), kind=kOutput, calls=%fused_computation.33 | convolution fusion | flops 3222011904 | bytes 8912896 | tf_op jit(solution)/shard_map/td,dsc->tsc/dot_general | solution.py:22
  131.3 1.7 collective-permute-start
  133.0 0.8 collective-permute-done
  133.8 0.3 maximum_convert_fusion
  134.1 2.6 multiply_add_fusion
  136.8 1.2 fusion.25
  137.9 2.9 multiply_reduce_fusion
  140.8 1.3 collective-permute-start.1
  142.1 4.1 %collective-permute-done.1 = f32[6,3,256]{2,0,1:T(8,128)S(1)} collective-permute-done((f32[6,3,256]{2,0,1:T(8,128)S(1)}, f32[6,3,256]{2,0,1:T(8,128)S(1)}, u32[]{:S(2)}, u32[]{:S(2)}) %collective-permute-start.1) | collective-permute-done | bytes 18464 | tf_op jit(solution)/shard_map/ppermute | solution.py:10
  146.2 0.2 pad_maximum_fusion
  146.4 2.7 fusion.8
  149.1 5.1 %bitcast_convert_fusion = bf16[1024,2048]{1,0:T(8,128)(2,1)} fusion(bf16[1024,3,256]{2,0,1:T(8,128)(2,1)S(1)} %fusion.8, bf16[2048,3,256]{2,0,1:T(8,128)(2,1)S(1)} %copy-done.3), kind=kOutput, calls=%fused_computation | convolution fusion | flops 3223322624 | bytes 8912896 | tf_op jit(solution)/shard_map/tsc,dsc->td/dot_general | solution.py:53
  154.2 0.0 reduce-scatter.3.cloned.1.call-update
  154.2 0.2 reduce-scatter.5.cloned.1.call-start
  154.5 7.5 %fusion.4 = bf16[2048,3,256]{2,0,1:T(8,128)(2,1)} fusion(bf16[1024,3,256]{2,0,1:T(8,128)(2,1)S(1)} %fusion.8, bf16[1024,2048]{1,0:T(8,128)(2,1)} %all-gather.3.cloned.1.call-done), kind=kOutput, calls=%fused_computation.5 | convolution fusion | flops 3222798336 | bytes 8912896 | tf_op jit(solution)/shard_map/td,tsc->dsc/dot_general | solution.py:59
  162.0 0.0 reduce-scatter.5.cloned.1.call-update
  162.1 49.9 %reduce-scatter.3.cloned.1.call-done = bf16[128,2048]{1,0:T(8,128)(2,1)} async-done(((bf16[1024,2048]{1,0:T(8,128)(2,1)}), bf16[128,2048]{1,0:T(8,128)(2,1)}) %reduce-scatter.3.cloned.1.call-update) | async-done | bytes 524304 | tf_op jit(solution)/shard_map/reduce_scatter | solution.py:56
  212.0 1.4 fusion.29
  213.4 144.5 %all-reduce = (f32[3,7,256]{2,0,1:T(4,128)S(1)}, f32[2048]{0:T(1024)S(1)}) all-reduce(f32[3,7,256]{2,0,1:T(4,128)S(1)} %constant_dynamic-update-slice_fusion, f32[2048]{0:T(1024)S(1)} %get-tuple-element.17), channel_id=1, replica_groups=mesh['dp'=32,'tensor'=8] {'dp'}, use_global_device_ids=true, to_apply=%region_11.0 | all-reduce | flops 7424 | bytes 59392 | tf_op jit(solution)/shard_map/psum | solution.py:70
  357.9 0.6 copy.12
  358.5 18.0 %psum.23 = f32[2048]{0:T(1024)} all-reduce(f32[2048]{0:T(1024)S(1)} %get-tuple-element.20), channel_id=1, replica_groups=mesh['dp'=32,'tensor'=8] {'tensor'}, use_global_device_ids=true, to_apply=%region_14.0 | all-reduce | flops 2048 | bytes 16384 | tf_op jit(solution)/shard_map/psum | solution.py:73
  376.5 2.2 fusion.23
  (24 shorter events, 0.1 us)
Async XLA Ops:
  7.2 62.2 %all-gather.5.cloned.1.call-start = ((), (), s32[]{:S(2)}) async-start(), calls=%async_computation.3 | async-start | bytes 3244032 | tf_op jit(solution)/shard_map/all_gather | solution.py:19
  7.9 116.8 %all-gather.3.cloned.1.call-start = ((), (), s32[]{:S(2)}) async-start(), calls=%async_computation.2 | async-start | bytes 4718592 | tf_op jit(solution)/shard_map/all_gather | solution.py:20
  11.2 200.7 %reduce-scatter.3.cloned.1.call-start = ((), (), s32[]{:S(2)}) async-start(), calls=%async_computation.4 | async-start | bytes 4718592 | tf_op jit(solution)/shard_map/reduce_scatter | solution.py:56
  131.3 2.6 collective-permute-start
  134.1 2.6 copy-start.1
  140.8 5.4 %collective-permute-start.1 = (f32[6,3,256]{2,0,1:T(8,128)S(1)}, f32[6,3,256]{2,0,1:T(8,128)S(1)}, u32[]{:S(2)}, u32[]{:S(2)}) collective-permute-start(f32[6,3,256]{2,0,1:T(8,128)S(1)} %slice.131), channel_id=1, source_target_pairs={{8,0},{16,8},{24,16},{32,24},{40,32},{48,40},{56,48},{64,56},{72,6... | collective-permute-start | bytes 55304 | tf_op jit(solution)/shard_map/ppermute | solution.py:10
  146.4 2.7 copy-start.3
  154.2 224.4 %reduce-scatter.5.cloned.1.call-start = ((), (), s32[]{:S(2)}) async-start(), calls=%async_computation.5 | async-start | bytes 3244032 | tf_op jit(solution)/shard_map/reduce_scatter | solution.py:62
  162.0 50.0 %copy-start = (bf16[128,2048]{1,0:T(8,128)(2,1)S(1)}, bf16[128,2048]{1,0:T(8,128)(2,1)}, u32[]{:S(2)}) copy-start(bf16[128,2048]{1,0:T(8,128)(2,1)} %param.5) | copy-start | bytes 1572868
  162.0 50.0 %copy-start.2 = (f32[2048]{0:T(1024)S(1)}, f32[2048]{0:T(1024)}, u32[]{:S(2)}) copy-start(f32[2048]{0:T(1024)} %param.6) | copy-start | bytes 24580
Sparse Core Ops, SparseCore 0:
  10.7 58.6 all-gather.4
  71.7 52.9 all-gather.2
  154.4 57.5 reduce-scatter.2
  216.3 94.9 reduce-scatter.4
